TPU v7x, 256 devices: a whole 4x4x8 slice. The times are simulated.
256 devices in a mesh: band: 2 (over y_hi), domain: 128 (over y_lo, x, z, core).
Axes of the slice: x: 4, y: 4 (y_hi: 2, y_lo: 2; y = y_hi * 2 + y_lo), z: 8, core: 2. Of those that a mesh axis runs over, the one named last changes fastest.
Arguments:
- targets: float32 [4, 36864, 192], P('band', 'domain'), may hold values from -5 to 5
- partner_pool: bfloat16 [64, 36864, 192], P('band', 'domain'), may hold values from -5 to 5
- owners: int32 [2], replicated, may hold values from 0 to 1, as said below
- warm_start: bfloat16 [2, 8, 4, 36864, 192], P(None, None, 'band', 'domain'), may hold values from -6 to 6
Outputs:
- exchange: float32 [4, 36864, 192], P('band', 'domain')
Inputs may be any that keep to these rules, and one draw needn't show every extreme that they name: The 2 broadcast blocks have distinct owners.
All inputs are finite; a program needn't handle non-finite values.
Results may differ from a plain program's by a relative error of at most 0.0006.
Values may be sent and summed in bfloat16 or wider, within the bound.
No kernel may reach another device: no remote copies, remote signals or barrier semaphores. Data moves between devices by JAX's collectives and lax.ppermute only.
A program may use at most 192 MiB of HBM per device.

v0:
```python
import math
import jax
import jax.numpy as jnp
from jax import lax
from jax.sharding import PartitionSpec as P

ORB = 8
STEPS = 2
SWEEPS = 3
GX = 192
GY = 192
GZ = 192
coupling = 4.0 * math.pi


def spread(block, axis, owner):
    block = jnp.where(lax.axis_index(axis) == owner, block, jnp.zeros_like(block))
    return lax.psum(block, axis)


def padded(block, sides, width):
    for axis, dim in sides:
        count = lax.axis_size(axis)
        forward = [(i, i + 1) for i in range(count - 1)]
        forward.append((count - 1, 0))
        backward = [(target, source) for source, target in forward]
        low = lax.ppermute(
            lax.slice_in_dim(block, block.shape[dim] - width, None, axis=dim), axis, forward
        )
        high = lax.ppermute(lax.slice_in_dim(block, 0, width, axis=dim), axis, backward)
        block = jnp.concatenate([low, block, high], axis=dim)
    return block


def row_sweep(widened, source, first_row):
    row_count = source.shape[1]
    line = GY
    centre = widened[:, line : line + row_count]
    beside = widened[:, :row_count] + widened[:, 2 * line : 2 * line + row_count]
    column = (first_row + jnp.arange(row_count, dtype=jnp.int32)) % line
    at_end = (column == line - 1)[None, :, None]
    at_start = (column == 0)[None, :, None]
    upper = jnp.where(
        at_end, widened[:, 1 : row_count + 1], widened[:, line + 1 : line + row_count + 1]
    )
    lower = jnp.where(
        at_start,
        widened[:, 2 * line - 1 : 2 * line - 1 + row_count],
        widened[:, line - 1 : line - 1 + row_count],
    )
    beside = beside + upper + lower + jnp.roll(centre, 1, 2) + jnp.roll(centre, -1, 2)
    return (beside + coupling * source) / 6.0


def fetch_block(partner_pool, owners, block_index):
    own_block = partner_pool[block_index * ORB : (block_index + 1) * ORB]
    return spread(own_block, "band", owners[block_index]).astype(jnp.float32)


def pair_products(partner, targets):
    density = partner[:, None] * targets[None]
    return (density, jnp.sum(density, axis=(2, 3)))


def solve_block(partner, density, mean_value, warm_block, first_row):
    block_width = partner.shape[0]
    target_count = density.shape[1]
    pair_count = block_width * target_count
    planes = density.shape[2:]
    source = density.reshape((pair_count,) + planes) - mean_value.reshape(pair_count, 1, 1)
    potential = warm_block.reshape((pair_count,) + planes).astype(jnp.float32)
    for sweep_index in range(SWEEPS):
        widened = padded(potential.astype(jnp.bfloat16), (("domain", 1),), GY).astype(
            potential.dtype
        )
        potential = row_sweep(widened, source, first_row)
    potential = potential.reshape((block_width, target_count) + planes)
    return jnp.sum(potential * partner[:, None], axis=0)


def body(targets, partner_pool, owners, warm_start):
    row_count = targets.shape[1]
    first_row = lax.axis_index("domain") * row_count
    cell_count = GX * GY * GZ
    exchange = jnp.zeros(targets.shape, jnp.float32)
    for block_index in range(STEPS):
        partner = fetch_block(partner_pool, owners, block_index)
        density, local_sums = pair_products(partner, targets)
        totals = lax.psum(local_sums, "domain")
        exchange = exchange - solve_block(
            partner, density, totals / cell_count, warm_start[block_index], first_row
        )
    return exchange


def solution(mesh):
    return jax.shard_map(
        body,
        mesh=mesh,
        in_specs=(
            P("band", "domain", None),
            P("band", "domain", None),
            P(),
            P(None, None, "band", "domain", None),
        ),
        out_specs=P("band", "domain", None),
        check_vma=False,
    )
```

profile of v0, /device:TPU:8, one launch (start us, length us, event | category | flops | bytes accessed | tf_op | source)
XLA Modules:
  0.0 645.0 jit_solution(16177434050569279853)
XLA Ops:
  6.5 2.7 fusion.59
  9.2 2.1 fusion.62
  11.4 0.0 collective-permute-start
  11.4 7.4 %collective-permute-start.1 = (bf16[16,192,192]{2,1,0:T(8,128)(2,1)}, bf16[16,192,192]{2,1,0:T(8,128)(2,1)}, u32[]{:S(2)}, u32[]{:S(2)}) collective-permute-start(bf16[16,192,192]{2,1,0:T(8,128)(2,1)} %get-tuple-element.46), channel_id=1, source_target_pairs={{1,0},{2,1},{3,2},{4,3},{5,4},{6,5},{7,6},{8,7},{9,8},{10,9},{11,1... | collective-permute-start | bytes 3538952 | tf_op jit(solution)/shard_map/ppermute | solution.py:30
  18.7 1.5 fusion.65
  20.2 0.0 collective-permute-start.6
  20.2 6.5 %collective-permute-start.7 = (bf16[16,192,192]{2,1,0:T(8,128)(2,1)S(1)}, bf16[16,192,192]{2,1,0:T(8,128)(2,1)}, u32[]{:S(2)}, u32[]{:S(2)}) collective-permute-start(bf16[16,192,192]{2,1,0:T(8,128)(2,1)S(1)} %get-tuple-element.52), channel_id=1, source_target_pairs={{1,0},{2,1},{3,2},{4,3},{5,4},{6,5},{7,6},{8,7},{9,8},{10,9},{11,1... | collective-permute-start | bytes 3538952 | tf_op jit(solution)/shard_map/ppermute | solution.py:30
  26.7 0.6 fusion.66
  28.7 3.2 slice_select_fusion.13
  31.9 0.0 all-reduce.4.cloned.1.call-update
  31.9 5.2 collective-permute-done
  37.2 0.0 collective-permute-done.1
  37.2 4.5 maximum_convert_fusion
  41.7 3.5 fusion.52
  45.2 8.9 %collective-permute-done.6 = bf16[16,192,192]{2,1,0:T(8,128)(2,1)} collective-permute-done((bf16[16,192,192]{2,1,0:T(8,128)(2,1)}, bf16[16,192,192]{2,1,0:T(8,128)(2,1)}, u32[]{:S(2)}, u32[]{:S(2)}) %collective-permute-start.6) | collective-permute-done | bytes 1179680 | tf_op jit(solution)/shard_map/ppermute | solution.py:27
  54.1 0.0 collective-permute-done.7
  54.1 3.8 maximum_convert_fusion.3
  57.9 3.4 fusion.58
  61.3 10.6 %fusion.51 = (f32[16,288,191]{2,1,0:T(8,128)}, f32[16,288,191]{2,1,0:T(8,128)}) fusion(f32[16,672,192]{2,1,0:T(8,128)} %copy-done.3), kind=kLoop, calls=%fused_computation.90 | loop fusion | bytes 14082048 | tf_op jit(solution)/shard_map/jit(_roll_static)/slice | solution.py:51
  71.9 5.4 fusion.57
  77.3 43.5 %all-reduce.4.cloned.1.call-done = (bf16[8,288,192]{2,1,0:T(8,128)(2,1)}, bf16[8,288,192]{2,1,0:T(8,128)(2,1)}) async-done(((bf16[8,288,192]{2,1,0:T(8,128)(2,1)}, bf16[8,288,192]{2,1,0:T(8,128)(2,1)}), (bf16[8,288,192]{2,1,0:T(8,128)(2,1)}, bf16[8,288,192]{2,1,0:T(8,128)(2,1)})) %all-reduce.4.cloned.1.call-update) | async-done | bytes 1769488 | tf_op jit(solution)/shard_map/psum | solution.py:18
  120.8 1.5 convert_element_type.41
  122.3 2.3 convert_element_type.47
  124.7 4.9 fusion.42
  129.6 285.4 %all-reduce = (f32[8,2]{1,0:T(8,128)S(1)}, f32[8,2]{1,0:T(8,128)S(1)}) all-reduce(f32[8,2]{1,0:T(8,128)S(1)} %get-tuple-element.6, f32[8,2]{1,0:T(8,128)S(1)} %get-tuple-element.5), channel_id=1, replica_groups=mesh['band'=2,'domain'=128] {'domain'}, use_global_device_ids=true, to_apply=%region_6.7 | all-reduce | flops 32 | bytes 256 | tf_op jit(solution)/shard_map/psum | solution.py:89
  415.0 0.1 sub.26
  415.1 18.2 %fusion.38 = bf16[16,288,192]{2,1,0:T(8,128)(2,1)S(1)} fusion(f32[16,672,192]{2,1,0:T(8,128)} %copy-done.3, f32[16,288,191]{2,1,0:T(8,128)} %get-tuple-element.20, f32[16,288,1]{2,1,0:T(8,128)} %get-tuple-element.22, f32[16,288,1]{2,1,0:T(8,128)} %get-tuple-element.21, f32[16,288,191]{2,1,0:T(8,128)} %get-tuple-element.19, ...), kind=kLoop, calls=%fused_computation.60 | loop fusion | flops 12386304 | bytes 33620608 | tf_op jit(solution)/shard_map/convert_element_type | solution.py:73
  433.3 2.1 fusion.61
  435.5 0.2 collective-permute-start.2
  435.6 6.0 collective-permute-start.3
  441.6 0.1 sub.30
  441.7 19.7 %fusion.18 = bf16[16,288,192]{2,1,0:T(8,128)(2,1)} fusion(f32[16,672,192]{2,1,0:T(8,128)} %copy-done.2, f32[16,288,191]{2,1,0:T(8,128)} %get-tuple-element.32, f32[16,288,1]{2,1,0:T(8,128)} %get-tuple-element.34, f32[16,288,1]{2,1,0:T(8,128)} %get-tuple-element.33, f32[16,288,191]{2,1,0:T(8,128)} %get-tuple-element.31, ...), kind=kLoop, calls=%fused_computation.31 | loop fusion | flops 12386304 | bytes 33620608 | tf_op jit(solution)/shard_map/convert_element_type | solution.py:73
  461.3 3.9 fusion.64
  465.2 6.2 collective-permute-start.9
  471.4 0.0 collective-permute-done.2
  471.4 0.0 collective-permute-done.3
  471.4 3.8 maximum_convert_fusion.1
  475.2 3.6 fusion.50
  478.8 5.3 fusion.49
  484.1 5.4 collective-permute-done.8
  489.5 0.1 collective-permute-done.9
  489.6 3.3 maximum_convert_fusion.4
  493.0 5.8 fusion.55
  498.7 1.1 copy-done.4
  499.9 2.9 fusion.56
  502.8 18.2 %fusion.31 = bf16[16,288,192]{2,1,0:T(8,128)(2,1)S(1)} fusion(f32[16,672,192]{2,1,0:T(8,128)} %copy-done.5, f32[16,288,191]{2,1,0:T(8,128)} %get-tuple-element.16, f32[16,288,1]{2,1,0:T(8,128)} %get-tuple-element.18, f32[16,288,1]{2,1,0:T(8,128)} %get-tuple-element.17, f32[16,288,191]{2,1,0:T(8,128)} %get-tuple-element.15, ...), kind=kLoop, calls=%fused_computation.50 | loop fusion | flops 12386304 | bytes 33620608 | tf_op jit(solution)/shard_map/convert_element_type | solution.py:73
  521.1 2.1 fusion.60
  523.2 6.4 collective-permute-start.5
  529.6 19.5 %fusion.11 = bf16[16,288,192]{2,1,0:T(8,128)(2,1)} fusion(f32[16,672,192]{2,1,0:T(8,128)} %copy-done.4, f32[16,288,191]{2,1,0:T(8,128)} %get-tuple-element.28, f32[16,288,1]{2,1,0:T(8,128)} %get-tuple-element.30, f32[16,288,1]{2,1,0:T(8,128)} %get-tuple-element.29, f32[16,288,191]{2,1,0:T(8,128)} %get-tuple-element.27, ...), kind=kLoop, calls=%fused_computation.21 | loop fusion | flops 12386304 | bytes 33620608 | tf_op jit(solution)/shard_map/convert_element_type | solution.py:73
  549.1 3.9 fusion.63
  553.0 6.0 collective-permute-start.11
  559.0 3.8 maximum_convert_fusion.2
  562.7 3.3 fusion.48
  566.1 5.3 fusion.47
  571.4 5.8 collective-permute-done.10
  577.3 3.3 maximum_convert_fusion.5
  580.6 5.8 fusion.53
  586.4 1.1 copy-done.1
  587.5 3.0 fusion.54
  590.5 20.2 %fusion.24 = f32[16,288,192]{2,1,0:T(8,128)} fusion(f32[16,672,192]{2,1,0:T(8,128)} %copy-done, f32[16,288,191]{2,1,0:T(8,128)} %get-tuple-element.12, f32[16,288,1]{2,1,0:T(8,128)} %get-tuple-element.14, f32[16,288,1]{2,1,0:T(8,128)} %get-tuple-element.13, f32[16,288,191]{2,1,0:T(8,128)} %get-tuple-element.11, f32[8,2,288,192]{3,2,1,0:T(8,128)} %get-tuple-element.39, ...), kind=kLoop, calls=%fused_computation.40 | loop fusion | flops 11501568 | bytes 35390080 | tf_op jit(solution)/shard_map/div | solution.py:52
  610.7 3.0 multiply_reduce_fusion.1
  613.7 20.0 %fusion.4 = f32[16,288,192]{2,1,0:T(8,128)} fusion(f32[16,672,192]{2,1,0:T(8,128)} %copy-done.1, f32[16,288,191]{2,1,0:T(8,128)} %get-tuple-element.24, f32[16,288,1]{2,1,0:T(8,128)} %get-tuple-element.26, f32[16,288,1]{2,1,0:T(8,128)} %get-tuple-element.25, f32[16,288,191]{2,1,0:T(8,128)} %get-tuple-element.23, f32[8,2,288,192]{3,2,1,0:T(8,128)} %get-tuple-element.40, ...), kind=kLoop, calls=%fused_computation.11 | loop fusion | flops 11501568 | bytes 35390080 | tf_op jit(solution)/shard_map/div | solution.py:52
  633.7 3.0 multiply_reduce_fusion
  636.7 0.9 subtract_subtract_fusion
  (40 shorter events, 0.1 us)
Async XLA Ops:
  6.5 114.3 %all-reduce.4.cloned.1.call-start = ((), (), s32[]{:S(2)}) async-start(), calls=%async_computation | async-start | bytes 4718592 | tf_op jit(solution)/shard_map/psum | solution.py:18
  9.2 11.0 %copy-start.8 = (bf16[1,8,2,288,192]{4,3,2,1,0:T(8,128)(2,1)}, bf16[1,8,2,288,192]{4,3,2,1,0:T(8,128)(2,1)S(1)}, u32[]{:S(2)}) copy-start(bf16[1,8,2,288,192]{4,3,2,1,0:T(8,128)(2,1)S(1)} %get-tuple-element.36) | copy-start | bytes 5308420
  9.2 11.0 %copy-start.9 = (bf16[1,8,2,288,192]{4,3,2,1,0:T(8,128)(2,1)}, bf16[1,8,2,288,192]{4,3,2,1,0:T(8,128)(2,1)S(1)}, u32[]{:S(2)}) copy-start(bf16[1,8,2,288,192]{4,3,2,1,0:T(8,128)(2,1)S(1)} %get-tuple-element.35) | copy-start | bytes 5308420
  11.4 15.3 %copy-start.15 = (s32[2]{0:T(128)S(1)}, s32[2]{0:T(128)}, u32[]{:S(2)}) copy-start(s32[2]{0:T(128)} %param.6) | copy-start | bytes 28
  11.4 25.8 %collective-permute-start = (bf16[16,192,192]{2,1,0:T(8,128)(2,1)}, bf16[16,192,192]{2,1,0:T(8,128)(2,1)}, u32[]{:S(2)}, u32[]{:S(2)}) collective-permute-start(bf16[16,192,192]{2,1,0:T(8,128)(2,1)} %get-tuple-element.45), channel_id=1, source_target_pairs={{0,1},{1,2},{2,3},{3,4},{4,5},{5,6},{6,7},{7,8},{8,9},{9,10},{10,1... | collective-permute-start | bytes 3538952 | tf_op jit(solution)/shard_map/ppermute | solution.py:27
  11.4 25.8 %collective-permute-start.1 = (bf16[16,192,192]{2,1,0:T(8,128)(2,1)}, bf16[16,192,192]{2,1,0:T(8,128)(2,1)}, u32[]{:S(2)}, u32[]{:S(2)}) collective-permute-start(bf16[16,192,192]{2,1,0:T(8,128)(2,1)} %get-tuple-element.46), channel_id=1, source_target_pairs={{1,0},{2,1},{3,2},{4,3},{5,4},{6,5},{7,6},{8,7},{9,8},{10,9},{11,1... | collective-permute-start | bytes 3538952 | tf_op jit(solution)/shard_map/ppermute | solution.py:30
  20.2 33.9 %collective-permute-start.6 = (bf16[16,192,192]{2,1,0:T(8,128)(2,1)}, bf16[16,192,192]{2,1,0:T(8,128)(2,1)}, u32[]{:S(2)}, u32[]{:S(2)}) collective-permute-start(bf16[16,192,192]{2,1,0:T(8,128)(2,1)} %get-tuple-element.51), channel_id=1, source_target_pairs={{0,1},{1,2},{2,3},{3,4},{4,5},{5,6},{6,7},{7,8},{8,9},{9,10},{10,1... | collective-permute-start | bytes 3538952 | tf_op jit(solution)/shard_map/ppermute | solution.py:27
  20.2 33.9 %collective-permute-start.7 = (bf16[16,192,192]{2,1,0:T(8,128)(2,1)S(1)}, bf16[16,192,192]{2,1,0:T(8,128)(2,1)}, u32[]{:S(2)}, u32[]{:S(2)}) collective-permute-start(bf16[16,192,192]{2,1,0:T(8,128)(2,1)S(1)} %get-tuple-element.52), channel_id=1, source_target_pairs={{1,0},{2,1},{3,2},{4,3},{5,4},{6,5},{7,6},{8,7},{9,8},{10,9},{11,1... | collective-permute-start | bytes 3538952 | tf_op jit(solution)/shard_map/ppermute | solution.py:30
  41.7 12.4 %copy-start.3 = (f32[16,672,192]{2,1,0:T(8,128)}, f32[16,672,192]{2,1,0:T(8,128)S(1)}, u32[]{:S(2)}) copy-start(f32[16,672,192]{2,1,0:T(8,128)S(1)} %maximum_convert_fusion) | copy-start | bytes 24772612
  57.9 14.0 %copy-start.2 = (f32[16,672,192]{2,1,0:T(8,128)}, f32[16,672,192]{2,1,0:T(8,128)S(1)}, u32[]{:S(2)}) copy-start(f32[16,672,192]{2,1,0:T(8,128)S(1)} %maximum_convert_fusion.3) | copy-start | bytes 24772612
  77.3 47.4 %copy-start.14 = (f32[2,288,192]{2,1,0:T(8,128)S(1)}, f32[2,288,192]{2,1,0:T(8,128)}, u32[]{:S(2)}) copy-start(f32[2,288,192]{2,1,0:T(8,128)} %param.4) | copy-start | bytes 1327108
  122.3 7.2 %copy-start.12 = (f32[8,288,192]{2,1,0:T(8,128)}, f32[8,288,192]{2,1,0:T(8,128)S(1)}, u32[]{:S(2)}) copy-start(f32[8,288,192]{2,1,0:T(8,128)S(1)} %convert_element_type.41) | copy-start | bytes 5308420
  124.7 4.9 copy-start.10
  433.3 28.0 %copy-start.6 = (bf16[16,288,192]{2,1,0:T(8,128)(2,1)}, bf16[16,288,192]{2,1,0:T(8,128)(2,1)S(1)}, u32[]{:S(2)}) copy-start(bf16[16,288,192]{2,1,0:T(8,128)(2,1)S(1)} %fusion.38) | copy-start | bytes 5308420
  435.5 35.9 %collective-permute-start.2 = (bf16[16,192,192]{2,1,0:T(8,128)(2,1)}, bf16[16,192,192]{2,1,0:T(8,128)(2,1)}, u32[]{:S(2)}, u32[]{:S(2)}) collective-permute-start(bf16[16,192,192]{2,1,0:T(8,128)(2,1)} %get-tuple-element.43), channel_id=1, source_target_pairs={{0,1},{1,2},{2,3},{3,4},{4,5},{5,6},{6,7},{7,8},{8,9},{9,10},{10,1... | collective-permute-start | bytes 3538952 | tf_op jit(solution)/shard_map/ppermute | solution.py:27
  435.6 35.8 %collective-permute-start.3 = (bf16[16,192,192]{2,1,0:T(8,128)(2,1)}, bf16[16,192,192]{2,1,0:T(8,128)(2,1)}, u32[]{:S(2)}, u32[]{:S(2)}) collective-permute-start(bf16[16,192,192]{2,1,0:T(8,128)(2,1)} %get-tuple-element.44), channel_id=1, source_target_pairs={{1,0},{2,1},{3,2},{4,3},{5,4},{6,5},{7,6},{8,7},{9,8},{10,9},{11,1... | collective-permute-start | bytes 3538952 | tf_op jit(solution)/shard_map/ppermute | solution.py:30
  465.2 24.3 %collective-permute-start.8 = (bf16[16,192,192]{2,1,0:T(8,128)(2,1)}, bf16[16,192,192]{2,1,0:T(8,128)(2,1)S(1)}, u32[]{:S(2)}, u32[]{:S(2)}) collective-permute-start(bf16[16,192,192]{2,1,0:T(8,128)(2,1)} %get-tuple-element.49), channel_id=1, source_target_pairs={{0,1},{1,2},{2,3},{3,4},{4,5},{5,6},{6,7},{7,8},{8,9},{9,10},{10,1... | collective-permute-start | bytes 3538952 | tf_op jit(solution)/shard_map/ppermute | solution.py:27
  465.2 24.4 %collective-permute-start.9 = (bf16[16,192,192]{2,1,0:T(8,128)(2,1)}, bf16[16,192,192]{2,1,0:T(8,128)(2,1)}, u32[]{:S(2)}, u32[]{:S(2)}) collective-permute-start(bf16[16,192,192]{2,1,0:T(8,128)(2,1)} %get-tuple-element.50), channel_id=1, source_target_pairs={{1,0},{2,1},{3,2},{4,3},{5,4},{6,5},{7,6},{8,7},{9,8},{10,9},{11,1... | collective-permute-start | bytes 3538952 | tf_op jit(solution)/shard_map/ppermute | solution.py:30
  475.2 9.0 %copy-start.5 = (f32[16,672,192]{2,1,0:T(8,128)}, f32[16,672,192]{2,1,0:T(8,128)S(1)}, u32[]{:S(2)}) copy-start(f32[16,672,192]{2,1,0:T(8,128)S(1)} %maximum_convert_fusion.1) | copy-start | bytes 24772612
  492.9 6.9 %copy-start.4 = (f32[16,672,192]{2,1,0:T(8,128)}, f32[16,672,192]{2,1,0:T(8,128)S(1)}, u32[]{:S(2)}) copy-start(f32[16,672,192]{2,1,0:T(8,128)S(1)} %maximum_convert_fusion.4) | copy-start | bytes 24772612
  521.1 28.0 %copy-start.7 = (bf16[16,288,192]{2,1,0:T(8,128)(2,1)}, bf16[16,288,192]{2,1,0:T(8,128)(2,1)S(1)}, u32[]{:S(2)}) copy-start(bf16[16,288,192]{2,1,0:T(8,128)(2,1)S(1)} %fusion.31) | copy-start | bytes 5308420
  523.2 35.8 %collective-permute-start.4 = (bf16[16,192,192]{2,1,0:T(8,128)(2,1)}, bf16[16,192,192]{2,1,0:T(8,128)(2,1)}, u32[]{:S(2)}, u32[]{:S(2)}) collective-permute-start(bf16[16,192,192]{2,1,0:T(8,128)(2,1)} %get-tuple-element.41), channel_id=1, source_target_pairs={{0,1},{1,2},{2,3},{3,4},{4,5},{5,6},{6,7},{7,8},{8,9},{9,10},{10,1... | collective-permute-start | bytes 3538952 | tf_op jit(solution)/shard_map/ppermute | solution.py:27
  523.2 35.8 %collective-permute-start.5 = (bf16[16,192,192]{2,1,0:T(8,128)(2,1)}, bf16[16,192,192]{2,1,0:T(8,128)(2,1)}, u32[]{:S(2)}, u32[]{:S(2)}) collective-permute-start(bf16[16,192,192]{2,1,0:T(8,128)(2,1)} %get-tuple-element.42), channel_id=1, source_target_pairs={{1,0},{2,1},{3,2},{4,3},{5,4},{6,5},{7,6},{8,7},{9,8},{10,9},{11,1... | collective-permute-start | bytes 3538952 | tf_op jit(solution)/shard_map/ppermute | solution.py:30
  553.0 24.3 %collective-permute-start.10 = (bf16[16,192,192]{2,1,0:T(8,128)(2,1)}, bf16[16,192,192]{2,1,0:T(8,128)(2,1)S(1)}, u32[]{:S(2)}, u32[]{:S(2)}) collective-permute-start(bf16[16,192,192]{2,1,0:T(8,128)(2,1)} %get-tuple-element.47), channel_id=1, source_target_pairs={{0,1},{1,2},{2,3},{3,4},{4,5},{5,6},{6,7},{7,8},{8,9},{9,10},{10,1... | collective-permute-start | bytes 3538952 | tf_op jit(solution)/shard_map/ppermute | solution.py:27
  553.0 24.3 %collective-permute-start.11 = (bf16[16,192,192]{2,1,0:T(8,128)(2,1)}, bf16[16,192,192]{2,1,0:T(8,128)(2,1)}, u32[]{:S(2)}, u32[]{:S(2)}) collective-permute-start(bf16[16,192,192]{2,1,0:T(8,128)(2,1)} %get-tuple-element.48), channel_id=1, source_target_pairs={{1,0},{2,1},{3,2},{4,3},{5,4},{6,5},{7,6},{8,7},{9,8},{10,9},{11,1... | collective-permute-start | bytes 3538952 | tf_op jit(solution)/shard_map/ppermute | solution.py:30
  562.7 8.7 %copy-start = (f32[16,672,192]{2,1,0:T(8,128)}, f32[16,672,192]{2,1,0:T(8,128)S(1)}, u32[]{:S(2)}) copy-start(f32[16,672,192]{2,1,0:T(8,128)S(1)} %maximum_convert_fusion.2) | copy-start | bytes 24772612
  580.6 6.9 %copy-start.1 = (f32[16,672,192]{2,1,0:T(8,128)}, f32[16,672,192]{2,1,0:T(8,128)S(1)}, u32[]{:S(2)}) copy-start(f32[16,672,192]{2,1,0:T(8,128)S(1)} %maximum_convert_fusion.5) | copy-start | bytes 24772612
  590.5 20.2 %copy-start.13 = (f32[8,288,192]{2,1,0:T(8,128)S(1)}, f32[8,288,192]{2,1,0:T(8,128)}, u32[]{:S(2)}) copy-start(f32[8,288,192]{2,1,0:T(8,128)} %copy-done.12) | copy-start | bytes 5308420
  613.7 20.0 %copy-start.11 = (f32[8,288,192]{2,1,0:T(8,128)S(1)}, f32[8,288,192]{2,1,0:T(8,128)}, u32[]{:S(2)}) copy-start(f32[8,288,192]{2,1,0:T(8,128)} %copy-done.10) | copy-start | bytes 5308420
Sparse Core Ops, SparseCore 0:
  32.0 88.7 all-reduce.3
where the time goes:
time: 649 us; the launch traced here: 645 us
  blocking collectives  285 us (44%)
  other arithmetic  157 us (24%)
  local copies, waits for them, and re-layouts  79.5 us (12%)
  waiting for transfers between devices  69.1 us (11%)
  starting transfers between devices  38.4 us (6%)
  between operations  15.5 us (2%)
    psum x1, blocking collectives, body(): totals = lax.psum(local_sums, 'domain')  285 us
    convert_element_type x4, other arithmetic, solve_block(): potential.astype(jnp.bfloat16)  75.7 us
    slice x12, local copies, waits for them, and re-layouts, row_sweep(): jnp.roll(centre, -1, 2)  58 us
    psum x1, waiting for transfers between devices, spread(): return lax.psum(block, axis)  43.5 us
    div x2, other arithmetic, row_sweep(): return (beside + coupling * source) / 6.0  40.2 us
    ppermute x6, starting transfers between devices, padded(): lax.ppermute(lax.slice_in_dim(block, 0, width, axis=dim), axis, backward)  38.3 us
    ppermute x6, waiting for transfers between devices, padded(): lax.ppermute(lax.slice_in_dim(block, block.shape[dim] - width, None, axis...  25.4 us
    convert_element_type x6, other arithmetic, solve_block(): padded(potential.astype(jnp.bfloat16), (('domain', 1),), GY)  22.4 us
  transfers between devices with their start and end apart: 13, of which 6 were waited for; matrix products, arithmetic and copies ran while one was open for 17% of the time, Pallas kernels for 0%

commit v1 on v0

--- a/solution.py
+++ b/solution.py
@@ -86,7 +86,8 @@
     for block_index in range(STEPS):
         partner = fetch_block(partner_pool, owners, block_index)
         density, local_sums = pair_products(partner, targets)
-        totals = lax.psum(local_sums, "domain")
+        pieces = lax.all_gather(local_sums, "domain")
+        totals = jnp.sum(pieces, axis=0)
         exchange = exchange - solve_block(
             partner, density, totals / cell_count, warm_start[block_index], first_row
         )

time: 649 us -> 687 us (1.059)
  blocking collectives: 285 us -> 325 us
    all_gather x0 -> x2, blocking collectives: none -> 325 us  [body(): pieces = lax.all_gather(local_sums, 'domain')]
    psum x1 -> x0, blocking collectives: 285 us -> none  [body(): totals = lax.psum(local_sums, 'domain')]
  transfers between devices with their start and end apart: 13 -> 13, of which waited for: 6 -> 6; matrix products, arithmetic and copies ran while one was open for 17% -> 16% of each run, Pallas kernels for 0% -> 0%
where the time goes in v1:
time: 687 us; the launch traced here: 683 us
  blocking collectives  325 us (47%)
  other arithmetic  156 us (23%)
  local copies, waits for them, and re-layouts  79.8 us (12%)
  waiting for transfers between devices  69.1 us (10%)
  starting transfers between devices  38.4 us (6%)
  between operations  15.1 us (2%)
    all_gather x2, blocking collectives, body(): pieces = lax.all_gather(local_sums, 'domain')  325 us
    convert_element_type x4, other arithmetic, solve_block(): potential.astype(jnp.bfloat16)  74.9 us
    slice x12, local copies, waits for them, and re-layouts, row_sweep(): jnp.roll(centre, -1, 2)  58.1 us
    psum x1, waiting for transfers between devices, spread(): return lax.psum(block, axis)  43.5 us
    div x2, other arithmetic, row_sweep(): return (beside + coupling * source) / 6.0  40.1 us
    ppermute x6, starting transfers between devices, padded(): lax.ppermute(lax.slice_in_dim(block, 0, width, axis=dim), axis, backward)  37.8 us
    ppermute x6, waiting for transfers between devices, padded(): lax.ppermute(lax.slice_in_dim(block, block.shape[dim] - width, None, axis...  25.4 us
    convert_element_type x6, other arithmetic, solve_block(): padded(potential.astype(jnp.bfloat16), (('domain', 1),), GY)  22.4 us
  transfers between devices with their start and end apart: 13, of which 6 were waited for; matrix products, arithmetic and copies ran while one was open for 16% of the time, Pallas kernels for 0%

profile of v1, /device:TPU:8, one launch (start us, length us, event | category | flops | bytes accessed | tf_op | source)
XLA Modules:
  0.0 683.5 jit_solution(17525781403238457589)
XLA Ops:
  6.5 2.7 fusion.59
  9.2 2.1 fusion.62
  11.4 7.4 %collective-permute-start.1 = (bf16[16,192,192]{2,1,0:T(8,128)(2,1)}, bf16[16,192,192]{2,1,0:T(8,128)(2,1)}, u32[]{:S(2)}, u32[]{:S(2)}) collective-permute-start(bf16[16,192,192]{2,1,0:T(8,128)(2,1)} %get-tuple-element.44), channel_id=1, source_target_pairs={{1,0},{2,1},{3,2},{4,3},{5,4},{6,5},{7,6},{8,7},{9,8},{10,9},{11,1... | collective-permute-start | bytes 3538952 | tf_op jit(solution)/shard_map/ppermute | solution.py:30
  18.8 1.5 fusion.65
  20.3 6.5 collective-permute-start.7
  26.7 0.6 fusion.66
  28.6 3.2 slice_select_fusion.13
  31.9 5.3 collective-permute-done
  37.2 4.5 maximum_convert_fusion
  41.7 3.5 fusion.52
  45.2 8.9 %collective-permute-done.6 = bf16[16,192,192]{2,1,0:T(8,128)(2,1)} collective-permute-done((bf16[16,192,192]{2,1,0:T(8,128)(2,1)}, bf16[16,192,192]{2,1,0:T(8,128)(2,1)}, u32[]{:S(2)}, u32[]{:S(2)}) %collective-permute-start.6) | collective-permute-done | bytes 1179680 | tf_op jit(solution)/shard_map/ppermute | solution.py:27
  54.1 3.8 maximum_convert_fusion.3
  57.9 3.5 fusion.58
  61.4 10.5 %fusion.51 = (f32[16,288,191]{2,1,0:T(8,128)}, f32[16,288,191]{2,1,0:T(8,128)}) fusion(f32[16,672,192]{2,1,0:T(8,128)} %copy-done.3), kind=kLoop, calls=%fused_computation.90 | loop fusion | bytes 14082048 | tf_op jit(solution)/shard_map/jit(_roll_static)/slice | solution.py:51
  71.9 5.4 fusion.57
  77.3 43.5 %all-reduce.3.cloned.1.call-done = (bf16[8,288,192]{2,1,0:T(8,128)(2,1)}, bf16[8,288,192]{2,1,0:T(8,128)(2,1)}) async-done(((bf16[8,288,192]{2,1,0:T(8,128)(2,1)}, bf16[8,288,192]{2,1,0:T(8,128)(2,1)}), (bf16[8,288,192]{2,1,0:T(8,128)(2,1)}, bf16[8,288,192]{2,1,0:T(8,128)(2,1)})) %all-reduce.3.cloned.1.call-update) | async-done | bytes 1769488 | tf_op jit(solution)/shard_map/psum | solution.py:18
  120.9 1.5 convert_element_type.41
  122.4 2.3 convert_element_type.47
  124.7 4.9 fusion.42
  129.7 157.3 %all-gather.2 = f32[128,8,2]{1,2,0:T(2,128)S(1)} all-gather(f32[1,8,2]{1,2,0:T(2,128)S(1)} %bitcast.34), channel_id=2, replica_groups=mesh['band'=2,'domain'=128] {'domain'}, dimensions={0}, use_global_device_ids=true | all-gather | bytes 8256 | tf_op jit(solution)/shard_map/all_gather | solution.py:89
  287.0 0.1 reduce_sum.55
  287.2 0.1 copy.6
  287.3 0.1 div.29
  287.3 17.9 %fusion.38 = bf16[16,288,192]{2,1,0:T(8,128)(2,1)S(1)} fusion(f32[16,672,192]{2,1,0:T(8,128)} %copy-done.3, f32[16,288,191]{2,1,0:T(8,128)} %get-tuple-element.18, f32[16,288,1]{2,1,0:T(8,128)} %get-tuple-element.20, f32[16,288,1]{2,1,0:T(8,128)} %get-tuple-element.19, f32[16,288,191]{2,1,0:T(8,128)} %get-tuple-element.17, ...), kind=kLoop, calls=%fused_computation.60 | loop fusion | flops 12386304 | bytes 33620608 | tf_op jit(solution)/shard_map/convert_element_type | solution.py:73
  305.2 2.1 fusion.61
  307.4 0.3 collective-permute-start.2
  307.7 5.6 collective-permute-start.3
  313.3 0.1 copy.7
  313.4 167.2 %all-gather.3 = f32[128,8,2]{1,2,0:T(2,128)S(1)} all-gather(f32[1,8,2]{1,2,0:T(2,128)S(1)} %bitcast.35), channel_id=3, replica_groups=mesh['band'=2,'domain'=128] {'domain'}, dimensions={0}, use_global_device_ids=true | all-gather | bytes 8256 | tf_op jit(solution)/shard_map/all_gather | solution.py:89
  480.6 0.1 reduce_sum.58
  480.8 0.1 copy.8
  480.9 0.1 div.34
  480.9 19.5 %fusion.18 = bf16[16,288,192]{2,1,0:T(8,128)(2,1)} fusion(f32[16,672,192]{2,1,0:T(8,128)} %copy-done.2, f32[16,288,191]{2,1,0:T(8,128)} %get-tuple-element.30, f32[16,288,1]{2,1,0:T(8,128)} %get-tuple-element.32, f32[16,288,1]{2,1,0:T(8,128)} %get-tuple-element.31, f32[16,288,191]{2,1,0:T(8,128)} %get-tuple-element.29, ...), kind=kLoop, calls=%fused_computation.31 | loop fusion | flops 12386304 | bytes 33620608 | tf_op jit(solution)/shard_map/convert_element_type | solution.py:73
  500.5 3.8 fusion.64
  504.3 0.3 collective-permute-start.8
  504.6 5.8 collective-permute-start.9
  510.5 3.8 maximum_convert_fusion.1
  514.2 3.6 fusion.50
  517.9 5.3 fusion.49
  523.2 5.4 collective-permute-done.8
  528.6 0.1 collective-permute-done.9
  528.7 3.3 maximum_convert_fusion.4
  532.0 5.8 fusion.55
  537.8 1.1 copy-done.4
  539.0 3.0 fusion.56
  541.9 18.0 %fusion.31 = bf16[16,288,192]{2,1,0:T(8,128)(2,1)S(1)} fusion(f32[16,672,192]{2,1,0:T(8,128)} %copy-done.5, f32[16,288,191]{2,1,0:T(8,128)} %get-tuple-element.14, f32[16,288,1]{2,1,0:T(8,128)} %get-tuple-element.16, f32[16,288,1]{2,1,0:T(8,128)} %get-tuple-element.15, f32[16,288,191]{2,1,0:T(8,128)} %get-tuple-element.13, ...), kind=kLoop, calls=%fused_computation.50 | loop fusion | flops 12386304 | bytes 33620608 | tf_op jit(solution)/shard_map/convert_element_type | solution.py:73
  559.9 2.1 fusion.60
  562.1 6.5 collective-permute-start.5
  568.6 19.5 %fusion.11 = bf16[16,288,192]{2,1,0:T(8,128)(2,1)} fusion(f32[16,672,192]{2,1,0:T(8,128)} %copy-done.4, f32[16,288,191]{2,1,0:T(8,128)} %get-tuple-element.26, f32[16,288,1]{2,1,0:T(8,128)} %get-tuple-element.28, f32[16,288,1]{2,1,0:T(8,128)} %get-tuple-element.27, f32[16,288,191]{2,1,0:T(8,128)} %get-tuple-element.25, ...), kind=kLoop, calls=%fused_computation.21 | loop fusion | flops 12386304 | bytes 33620608 | tf_op jit(solution)/shard_map/convert_element_type | solution.py:73
  588.1 3.9 fusion.63
  592.0 6.0 collective-permute-start.11
  597.9 3.8 maximum_convert_fusion.2
  601.7 3.3 fusion.48
  605.0 5.3 fusion.47
  610.4 5.9 collective-permute-done.10
  616.2 3.3 maximum_convert_fusion.5
  619.6 5.8 fusion.53
  625.4 1.1 copy-done.1
  626.5 3.0 fusion.54
  629.5 20.2 %fusion.24 = f32[16,288,192]{2,1,0:T(8,128)} fusion(f32[16,672,192]{2,1,0:T(8,128)} %copy-done, f32[16,288,191]{2,1,0:T(8,128)} %get-tuple-element.10, f32[16,288,1]{2,1,0:T(8,128)} %get-tuple-element.12, f32[16,288,1]{2,1,0:T(8,128)} %get-tuple-element.11, f32[16,288,191]{2,1,0:T(8,128)} %get-tuple-element.9, f32[8,2,288,192]{3,2,1,0:T(8,128)} %get-tuple-element.37, ...), kind=kLoop, calls=%fused_computation.40 | loop fusion | flops 11501568 | bytes 35390080 | tf_op jit(solution)/shard_map/div | solution.py:52
  649.6 3.0 multiply_reduce_fusion.1
  652.6 19.9 %fusion.4 = f32[16,288,192]{2,1,0:T(8,128)} fusion(f32[16,672,192]{2,1,0:T(8,128)} %copy-done.1, f32[16,288,191]{2,1,0:T(8,128)} %get-tuple-element.22, f32[16,288,1]{2,1,0:T(8,128)} %get-tuple-element.24, f32[16,288,1]{2,1,0:T(8,128)} %get-tuple-element.23, f32[16,288,191]{2,1,0:T(8,128)} %get-tuple-element.21, f32[8,2,288,192]{3,2,1,0:T(8,128)} %get-tuple-element.38, ...), kind=kLoop, calls=%fused_computation.11 | loop fusion | flops 11501568 | bytes 35390080 | tf_op jit(solution)/shard_map/div | solution.py:52
  672.5 3.0 multiply_reduce_fusion
  675.5 0.9 subtract_subtract_fusion
  (47 shorter events, 0.2 us)
Async XLA Ops:
  6.5 114.3 %all-reduce.3.cloned.1.call-start = ((), (), s32[]{:S(2)}) async-start(), calls=%async_computation | async-start | bytes 4718592 | tf_op jit(solution)/shard_map/psum | solution.py:18
  9.2 11.0 %copy-start.8 = (bf16[1,8,2,288,192]{4,3,2,1,0:T(8,128)(2,1)}, bf16[1,8,2,288,192]{4,3,2,1,0:T(8,128)(2,1)S(1)}, u32[]{:S(2)}) copy-start(bf16[1,8,2,288,192]{4,3,2,1,0:T(8,128)(2,1)S(1)} %get-tuple-element.34) | copy-start | bytes 5308420
  9.2 11.0 %copy-start.9 = (bf16[1,8,2,288,192]{4,3,2,1,0:T(8,128)(2,1)}, bf16[1,8,2,288,192]{4,3,2,1,0:T(8,128)(2,1)S(1)}, u32[]{:S(2)}) copy-start(bf16[1,8,2,288,192]{4,3,2,1,0:T(8,128)(2,1)S(1)} %get-tuple-element.33) | copy-start | bytes 5308420
  11.4 15.4 %copy-start.15 = (s32[2]{0:T(128)S(1)}, s32[2]{0:T(128)}, u32[]{:S(2)}) copy-start(s32[2]{0:T(128)} %param.6) | copy-start | bytes 28
  11.4 25.8 %collective-permute-start = (bf16[16,192,192]{2,1,0:T(8,128)(2,1)}, bf16[16,192,192]{2,1,0:T(8,128)(2,1)}, u32[]{:S(2)}, u32[]{:S(2)}) collective-permute-start(bf16[16,192,192]{2,1,0:T(8,128)(2,1)} %get-tuple-element.43), channel_id=1, source_target_pairs={{0,1},{1,2},{2,3},{3,4},{4,5},{5,6},{6,7},{7,8},{8,9},{9,10},{10,1... | collective-permute-start | bytes 3538952 | tf_op jit(solution)/shard_map/ppermute | solution.py:27
  11.4 25.8 %collective-permute-start.1 = (bf16[16,192,192]{2,1,0:T(8,128)(2,1)}, bf16[16,192,192]{2,1,0:T(8,128)(2,1)}, u32[]{:S(2)}, u32[]{:S(2)}) collective-permute-start(bf16[16,192,192]{2,1,0:T(8,128)(2,1)} %get-tuple-element.44), channel_id=1, source_target_pairs={{1,0},{2,1},{3,2},{4,3},{5,4},{6,5},{7,6},{8,7},{9,8},{10,9},{11,1... | collective-permute-start | bytes 3538952 | tf_op jit(solution)/shard_map/ppermute | solution.py:30
  20.3 33.9 %collective-permute-start.6 = (bf16[16,192,192]{2,1,0:T(8,128)(2,1)}, bf16[16,192,192]{2,1,0:T(8,128)(2,1)}, u32[]{:S(2)}, u32[]{:S(2)}) collective-permute-start(bf16[16,192,192]{2,1,0:T(8,128)(2,1)} %get-tuple-element.49), channel_id=1, source_target_pairs={{0,1},{1,2},{2,3},{3,4},{4,5},{5,6},{6,7},{7,8},{8,9},{9,10},{10,1... | collective-permute-start | bytes 3538952 | tf_op jit(solution)/shard_map/ppermute | solution.py:27
  20.3 33.9 %collective-permute-start.7 = (bf16[16,192,192]{2,1,0:T(8,128)(2,1)S(1)}, bf16[16,192,192]{2,1,0:T(8,128)(2,1)}, u32[]{:S(2)}, u32[]{:S(2)}) collective-permute-start(bf16[16,192,192]{2,1,0:T(8,128)(2,1)S(1)} %get-tuple-element.50), channel_id=1, source_target_pairs={{1,0},{2,1},{3,2},{4,3},{5,4},{6,5},{7,6},{8,7},{9,8},{10,9},{11,1... | collective-permute-start | bytes 3538952 | tf_op jit(solution)/shard_map/ppermute | solution.py:30
  41.7 12.4 %copy-start.3 = (f32[16,672,192]{2,1,0:T(8,128)}, f32[16,672,192]{2,1,0:T(8,128)S(1)}, u32[]{:S(2)}) copy-start(f32[16,672,192]{2,1,0:T(8,128)S(1)} %maximum_convert_fusion) | copy-start | bytes 24772612
  57.9 14.0 %copy-start.2 = (f32[16,672,192]{2,1,0:T(8,128)}, f32[16,672,192]{2,1,0:T(8,128)S(1)}, u32[]{:S(2)}) copy-start(f32[16,672,192]{2,1,0:T(8,128)S(1)} %maximum_convert_fusion.3) | copy-start | bytes 24772612
  77.3 47.4 %copy-start.14 = (f32[2,288,192]{2,1,0:T(8,128)S(1)}, f32[2,288,192]{2,1,0:T(8,128)}, u32[]{:S(2)}) copy-start(f32[2,288,192]{2,1,0:T(8,128)} %param.4) | copy-start | bytes 1327108
  122.3 7.2 %copy-start.12 = (f32[8,288,192]{2,1,0:T(8,128)}, f32[8,288,192]{2,1,0:T(8,128)S(1)}, u32[]{:S(2)}) copy-start(f32[8,288,192]{2,1,0:T(8,128)S(1)} %convert_element_type.41) | copy-start | bytes 5308420
  124.7 4.9 copy-start.10
  305.2 195.2 %copy-start.6 = (bf16[16,288,192]{2,1,0:T(8,128)(2,1)}, bf16[16,288,192]{2,1,0:T(8,128)(2,1)S(1)}, u32[]{:S(2)}) copy-start(bf16[16,288,192]{2,1,0:T(8,128)(2,1)S(1)} %fusion.38) | copy-start | bytes 5308420
  307.4 203.1 %collective-permute-start.2 = (bf16[16,192,192]{2,1,0:T(8,128)(2,1)}, bf16[16,192,192]{2,1,0:T(8,128)(2,1)}, u32[]{:S(2)}, u32[]{:S(2)}) collective-permute-start(bf16[16,192,192]{2,1,0:T(8,128)(2,1)} %get-tuple-element.41), channel_id=1, source_target_pairs={{0,1},{1,2},{2,3},{3,4},{4,5},{5,6},{6,7},{7,8},{8,9},{9,10},{10,1... | collective-permute-start | bytes 3538952 | tf_op jit(solution)/shard_map/ppermute | solution.py:27
  307.7 202.8 %collective-permute-start.3 = (bf16[16,192,192]{2,1,0:T(8,128)(2,1)}, bf16[16,192,192]{2,1,0:T(8,128)(2,1)}, u32[]{:S(2)}, u32[]{:S(2)}) collective-permute-start(bf16[16,192,192]{2,1,0:T(8,128)(2,1)} %get-tuple-element.42), channel_id=1, source_target_pairs={{1,0},{2,1},{3,2},{4,3},{5,4},{6,5},{7,6},{8,7},{9,8},{10,9},{11,1... | collective-permute-start | bytes 3538952 | tf_op jit(solution)/shard_map/ppermute | solution.py:30
  504.3 24.3 %collective-permute-start.8 = (bf16[16,192,192]{2,1,0:T(8,128)(2,1)}, bf16[16,192,192]{2,1,0:T(8,128)(2,1)S(1)}, u32[]{:S(2)}, u32[]{:S(2)}) collective-permute-start(bf16[16,192,192]{2,1,0:T(8,128)(2,1)} %get-tuple-element.47), channel_id=1, source_target_pairs={{0,1},{1,2},{2,3},{3,4},{4,5},{5,6},{6,7},{7,8},{8,9},{9,10},{10,1... | collective-permute-start | bytes 3538952 | tf_op jit(solution)/shard_map/ppermute | solution.py:27
  504.6 24.1 %collective-permute-start.9 = (bf16[16,192,192]{2,1,0:T(8,128)(2,1)}, bf16[16,192,192]{2,1,0:T(8,128)(2,1)}, u32[]{:S(2)}, u32[]{:S(2)}) collective-permute-start(bf16[16,192,192]{2,1,0:T(8,128)(2,1)} %get-tuple-element.48), channel_id=1, source_target_pairs={{1,0},{2,1},{3,2},{4,3},{5,4},{6,5},{7,6},{8,7},{9,8},{10,9},{11,1... | collective-permute-start | bytes 3538952 | tf_op jit(solution)/shard_map/ppermute | solution.py:30
  514.2 9.0 %copy-start.5 = (f32[16,672,192]{2,1,0:T(8,128)}, f32[16,672,192]{2,1,0:T(8,128)S(1)}, u32[]{:S(2)}) copy-start(f32[16,672,192]{2,1,0:T(8,128)S(1)} %maximum_convert_fusion.1) | copy-start | bytes 24772612
  532.0 6.9 %copy-start.4 = (f32[16,672,192]{2,1,0:T(8,128)}, f32[16,672,192]{2,1,0:T(8,128)S(1)}, u32[]{:S(2)}) copy-start(f32[16,672,192]{2,1,0:T(8,128)S(1)} %maximum_convert_fusion.4) | copy-start | bytes 24772612
  559.9 28.2 %copy-start.7 = (bf16[16,288,192]{2,1,0:T(8,128)(2,1)}, bf16[16,288,192]{2,1,0:T(8,128)(2,1)S(1)}, u32[]{:S(2)}) copy-start(bf16[16,288,192]{2,1,0:T(8,128)(2,1)S(1)} %fusion.31) | copy-start | bytes 5308420
  562.1 35.9 %collective-permute-start.4 = (bf16[16,192,192]{2,1,0:T(8,128)(2,1)}, bf16[16,192,192]{2,1,0:T(8,128)(2,1)}, u32[]{:S(2)}, u32[]{:S(2)}) collective-permute-start(bf16[16,192,192]{2,1,0:T(8,128)(2,1)} %get-tuple-element.39), channel_id=1, source_target_pairs={{0,1},{1,2},{2,3},{3,4},{4,5},{5,6},{6,7},{7,8},{8,9},{9,10},{10,1... | collective-permute-start | bytes 3538952 | tf_op jit(solution)/shard_map/ppermute | solution.py:27
  562.1 35.9 %collective-permute-start.5 = (bf16[16,192,192]{2,1,0:T(8,128)(2,1)}, bf16[16,192,192]{2,1,0:T(8,128)(2,1)}, u32[]{:S(2)}, u32[]{:S(2)}) collective-permute-start(bf16[16,192,192]{2,1,0:T(8,128)(2,1)} %get-tuple-element.40), channel_id=1, source_target_pairs={{1,0},{2,1},{3,2},{4,3},{5,4},{6,5},{7,6},{8,7},{9,8},{10,9},{11,1... | collective-permute-start | bytes 3538952 | tf_op jit(solution)/shard_map/ppermute | solution.py:30
  592.0 24.3 %collective-permute-start.10 = (bf16[16,192,192]{2,1,0:T(8,128)(2,1)}, bf16[16,192,192]{2,1,0:T(8,128)(2,1)S(1)}, u32[]{:S(2)}, u32[]{:S(2)}) collective-permute-start(bf16[16,192,192]{2,1,0:T(8,128)(2,1)} %get-tuple-element.45), channel_id=1, source_target_pairs={{0,1},{1,2},{2,3},{3,4},{4,5},{5,6},{6,7},{7,8},{8,9},{9,10},{10,1... | collective-permute-start | bytes 3538952 | tf_op jit(solution)/shard_map/ppermute | solution.py:27
  592.0 24.3 %collective-permute-start.11 = (bf16[16,192,192]{2,1,0:T(8,128)(2,1)}, bf16[16,192,192]{2,1,0:T(8,128)(2,1)}, u32[]{:S(2)}, u32[]{:S(2)}) collective-permute-start(bf16[16,192,192]{2,1,0:T(8,128)(2,1)} %get-tuple-element.46), channel_id=1, source_target_pairs={{1,0},{2,1},{3,2},{4,3},{5,4},{6,5},{7,6},{8,7},{9,8},{10,9},{11,1... | collective-permute-start | bytes 3538952 | tf_op jit(solution)/shard_map/ppermute | solution.py:30
  601.7 8.7 %copy-start = (f32[16,672,192]{2,1,0:T(8,128)}, f32[16,672,192]{2,1,0:T(8,128)S(1)}, u32[]{:S(2)}) copy-start(f32[16,672,192]{2,1,0:T(8,128)S(1)} %maximum_convert_fusion.2) | copy-start | bytes 24772612
  619.6 6.9 %copy-start.1 = (f32[16,672,192]{2,1,0:T(8,128)}, f32[16,672,192]{2,1,0:T(8,128)S(1)}, u32[]{:S(2)}) copy-start(f32[16,672,192]{2,1,0:T(8,128)S(1)} %maximum_convert_fusion.5) | copy-start | bytes 24772612
  629.5 20.2 %copy-start.13 = (f32[8,288,192]{2,1,0:T(8,128)S(1)}, f32[8,288,192]{2,1,0:T(8,128)}, u32[]{:S(2)}) copy-start(f32[8,288,192]{2,1,0:T(8,128)} %copy-done.12) | copy-start | bytes 5308420
  652.6 20.0 %copy-start.11 = (f32[8,288,192]{2,1,0:T(8,128)S(1)}, f32[8,288,192]{2,1,0:T(8,128)}, u32[]{:S(2)}) copy-start(f32[8,288,192]{2,1,0:T(8,128)} %copy-done.10) | copy-start | bytes 5308420
Sparse Core Ops, SparseCore 0:
  32.0 88.8 all-reduce.2
